TPU v7x, 32 devices: a whole 2x2x4 slice. The times are simulated.
32 devices in a mesh: cand: 2 (over core), test: 8 (over z, x), feat: 2 (over y).
Axes of the slice: x: 2, y: 2, z: 4, core: 2. Of those that a mesh axis runs over, the one named last changes fastest.
Arguments:
- x_test: float32 [32768, 256], P(('test', 'cand'), 'feat'), may hold values from -6 to 6
- x_cand: float32 [8192, 256], P(('cand', 'test'), 'feat'), may hold values from -6 to 6
- w_self: float32 [256, 256], replicated, may hold values from -0.375 to 0.375
- w_neigh: float32 [256, 256], replicated, may hold values from -1.5 to 1.5
- d_out: float32 [8192, 256], P(('cand', 'test'), 'feat'), may hold values from -6 to 6
- block_row: int32 [2, 8, 512], P('cand', 'test'), may hold values from 0 to 31, as said below
- block_col: int32 [2, 8, 512], P('cand', 'test'), may hold values from 0 to 31, as said below
- block_mask: int32 [2, 8, 512, 16, 128], P('cand', 'test'), may hold values from 0 to 255, as said below
- block_live: int32 [2, 8], P('cand', 'test'), may hold values from 170 to 512, as said below
Outputs:
- output: float32 [8192, 256], P(('cand', 'test'), 'feat')
- grad_w_self: float32 [256, 256], P('feat')
- grad_w_neigh: float32 [256, 256], P('feat')
- grad_x_cand: float32 [8192, 256], P(('cand', 'test'), 'feat')
- grad_x_test: float32 [32768, 256], P(('test', 'cand'), 'feat')
Inputs may be any that keep to these rules, and one draw needn't show every extreme that they name: `block_row`: within one device's list the 512 slots name distinct (row block, column block) positions. `block_col`: within one device's list the 512 slots name distinct (row block, column block) positions. `block_mask`: each word holds 8 bits. `block_live`: some device has all 512 slots live in every draw.
All inputs are finite; a program needn't handle non-finite values.
Results may differ from a plain program's by a relative error of at most 0.0003.
Values sent between devices are 32-bit elements; how exact they have to be, the bound alone decides.
No kernel may reach another device: no remote copies, remote signals or barrier semaphores. Data moves between devices by JAX's collectives and lax.ppermute only.
A program may use at most 64 MiB of HBM per device.

v0:
```python
import math
import jax
import jax.numpy as jnp
from jax import lax
from jax.sharding import PartitionSpec as P

HIGHEST = lax.Precision.HIGHEST


def unpack_masks(packed):
    shifts = jnp.arange(8, dtype=jnp.int32)
    bit_cube = jnp.bitwise_and(jnp.right_shift(packed[..., :, None, :], shifts[:, None]), 1)
    return bit_cube.reshape(packed.shape[:-2] + (packed.shape[-2] * 8, packed.shape[-1])).astype(
        jnp.float32
    )


def slot_loop(live_count, offset, stride, slot_total, step_fn, initial):
    group_size = 16
    usable = (live_count - offset + stride - 1) // stride
    group_count = (usable + group_size - 1) // group_size

    def one_group(group_index, running):
        raw_slots = offset + stride * (
            group_index * group_size + jnp.arange(group_size, dtype=jnp.int32)
        )
        weights = (raw_slots < live_count).astype(jnp.float32)
        safe_slots = jnp.minimum(raw_slots, slot_total - 1)
        return step_fn(running, safe_slots, weights)

    return lax.fori_loop(0, group_count, one_group, initial)


def aggregate(
    packed_masks,
    block_rows,
    block_cols,
    live_count,
    offset,
    stride,
    fetch_tiles,
    row_blocks,
    feature_count,
):
    block_edge = packed_masks.shape[-1]

    def step_fn(running, safe_slots, weights):
        row_totals, row_counts = running
        dense_masks = unpack_masks(packed_masks[safe_slots])
        feature_tiles = fetch_tiles(block_cols[safe_slots])
        products = jnp.einsum("gij,gjh->gih", dense_masks, feature_tiles, precision=HIGHEST)
        selector = (
            block_rows[safe_slots][:, None] == jnp.arange(row_blocks, dtype=jnp.int32)[None, :]
        ).astype(jnp.float32) * weights[:, None]
        row_totals = row_totals + jnp.einsum("gk,gih->kih", selector, products, precision=HIGHEST)
        row_counts = row_counts + jnp.einsum(
            "gk,gi->ki", selector, jnp.sum(dense_masks, axis=2), precision=HIGHEST
        )
        return (row_totals, row_counts)

    initial = (
        jnp.zeros((row_blocks, block_edge, feature_count), jnp.float32),
        jnp.zeros((row_blocks, block_edge), jnp.float32),
    )
    return slot_loop(live_count, offset, stride, packed_masks.shape[0], step_fn, initial)


def transpose_product(packed_masks, block_rows, block_cols, live_count, gradient_tiles, col_blocks):
    block_edge = packed_masks.shape[-1]

    def step_fn(running, safe_slots, weights):
        dense_masks = unpack_masks(packed_masks[safe_slots])
        picked = gradient_tiles[block_rows[safe_slots]]
        products = jnp.einsum("gji,gjh->gih", dense_masks, picked, precision=HIGHEST)
        selector = (
            block_cols[safe_slots][:, None] == jnp.arange(col_blocks, dtype=jnp.int32)[None, :]
        ).astype(jnp.float32) * weights[:, None]
        return running + jnp.einsum("gk,gih->kih", selector, products, precision=HIGHEST)

    initial = jnp.zeros((col_blocks, block_edge, gradient_tiles.shape[-1]), jnp.float32)
    return slot_loop(live_count, 0, 1, packed_masks.shape[0], step_fn, initial)


def local(x_test, x_cand, w_self, w_neigh, d_out, block_row, block_col, block_mask, block_live):
    packed_masks = block_mask.reshape(block_mask.shape[2:])
    block_rows = block_row.reshape(-1)
    block_cols = block_col.reshape(-1)
    live_count = block_live.reshape(())
    block_edge = packed_masks.shape[-1]
    cand_count = lax.axis_size("cand")
    test_count = lax.axis_size("test")
    feat_index = lax.axis_index("feat")
    half_width = x_cand.shape[1]
    row_blocks = x_cand.shape[0] * test_count // block_edge
    col_blocks = x_test.shape[0] * cand_count // block_edge
    panel = lax.all_gather(x_test, "cand", axis=0, tiled=True)
    feature_tiles = panel.reshape(col_blocks, block_edge, half_width)

    def fetch_tiles(chosen):
        return feature_tiles[chosen]

    row_totals, row_counts = aggregate(
        packed_masks, block_rows, block_cols, live_count, 0, 1, fetch_tiles, row_blocks, half_width
    )
    own_totals, degree = (
        lax.psum_scatter(
            row_totals.reshape(-1, half_width), "test", scatter_dimension=0, tiled=True
        ),
        lax.psum_scatter(row_counts.reshape(-1), "test", scatter_dimension=0, tiled=True),
    )
    aggregated = own_totals / (1.0 + degree)[:, None]
    self_cols = lax.dynamic_slice_in_dim(w_self, feat_index * half_width, half_width, 1)
    neigh_cols = lax.dynamic_slice_in_dim(w_neigh, feat_index * half_width, half_width, 1)
    self_rows = lax.dynamic_slice_in_dim(w_self, feat_index * half_width, half_width, 0)
    neigh_rows = lax.dynamic_slice_in_dim(w_neigh, feat_index * half_width, half_width, 0)
    cand_full, aggregated_full = (
        lax.all_gather(x_cand, "feat", axis=1, tiled=True),
        lax.all_gather(aggregated, "feat", axis=1, tiled=True),
    )
    pre_act = jnp.dot(cand_full, self_cols, precision=HIGHEST) + jnp.dot(
        aggregated_full, neigh_cols, precision=HIGHEST
    )
    output = jax.nn.silu(pre_act)
    sigmoid_z = jax.nn.sigmoid(pre_act)
    grad_pre = d_out * (sigmoid_z * (1.0 + pre_act * (1.0 - sigmoid_z)))
    grad_full = lax.all_gather(grad_pre, "feat", axis=1, tiled=True)
    self_part = jnp.einsum("rk,rh->kh", x_cand, grad_full, precision=HIGHEST)
    neigh_part = jnp.einsum("rk,rh->kh", aggregated, grad_full, precision=HIGHEST)
    self_sum, neigh_sum = lax.psum((self_part, neigh_part), ("cand", "test"))
    root_count = math.sqrt(x_cand.shape[0] * cand_count * test_count)
    grad_w_self = self_sum / root_count
    grad_w_neigh = neigh_sum / root_count
    grad_x_cand = jnp.dot(grad_full, self_rows.T, precision=HIGHEST)
    grad_agg = jnp.dot(grad_full, neigh_rows.T, precision=HIGHEST)
    lifted = grad_agg / (1.0 + degree)[:, None]
    gathered_rows = lax.all_gather(lifted, "test", axis=0, tiled=True)
    gradient_tiles = gathered_rows.reshape(row_blocks, block_edge, half_width)
    column_terms = transpose_product(
        packed_masks, block_rows, block_cols, live_count, gradient_tiles, col_blocks
    )
    grad_x_test = lax.psum_scatter(
        column_terms.reshape(-1, half_width), "cand", scatter_dimension=0, tiled=True
    )
    return (output, grad_w_self, grad_w_neigh, grad_x_cand, grad_x_test)


def solution(mesh):
    return jax.shard_map(
        local,
        mesh=mesh,
        in_specs=(
            P(("test", "cand"), "feat"),
            P(("cand", "test"), "feat"),
            P(),
            P(),
            P(("cand", "test"), "feat"),
            P("cand", "test", None),
            P("cand", "test", None),
            P("cand", "test", None, None, None),
            P("cand", "test"),
        ),
        out_specs=(
            P(("cand", "test"), "feat"),
            P("feat", None),
            P("feat", None),
            P(("cand", "test"), "feat"),
            P(("test", "cand"), "feat"),
        ),
        check_vma=False,
    )
```

profile of v0, /device:TPU:0, one launch (start us, length us, event | category | flops | bytes accessed | tf_op | source)
XLA Modules:
  0.0 1031.7 jit_solution(8891889499213554505)
XLA Ops:
  8.6 14.2 %all-gather.3.cloned.1.call-done = f32[4096,128]{1,0:T(8,128)} async-done(((f32[2048,128]{1,0:T(8,128)}), f32[4096,128]{1,0:T(8,128)}) %all-gather.3.cloned.1.call-update) | async-done | bytes 2097168 | tf_op jit(solution)/shard_map/all_gather | solution.py:96
  23.8 148.9 %while.22 = (s32[]{:T(128)}, f32[32,128,128]{2,0,1:T(8,128)S(1)}, f32[32,128]{1,0:T(8,128)}, s32[]{:T(128)}, s32[512]{0:T(512)S(1)}, /*index=5*/s32[]{:T(128)}, ...) while((s32[]{:T(128)}, f32[32,128,128]{2,0,1:T(8,128)S(1)}, ...), condition=%wide.region_2.3_spmd, body=%wide.region_0.2_spmd.sunk | while | flops 506468544 | bytes 10039669 | solution.py:31
  34.4 2.9 convolution_add_fusion.7
  47.9 2.9 convolution_add_fusion.7
  61.5 2.9 convolution_add_fusion.7
  75.0 2.9 convolution_add_fusion.7
  88.6 2.9 convolution_add_fusion.7
  102.1 2.9 convolution_add_fusion.7
  115.6 2.9 convolution_add_fusion.7
  129.2 2.9 convolution_add_fusion.7
  142.7 2.9 convolution_add_fusion.7
  156.2 2.9 convolution_add_fusion.7
  169.8 2.9 convolution_add_fusion.7
  177.6 9.2 all_gather.15
  187.5 321.7 %all-reduce = f32[4096]{0:T(1024)S(1)} all-reduce(f32[4096]{0:T(1024)} %bitcast.18), channel_id=3, replica_groups=mesh['cand'=2,'test'=8,'feat'=2] {'test'}, use_global_device_ids=true, to_apply=%region_4.5.clone | all-reduce | flops 4096 | bytes 32768
  509.3 20.2 %reduce-scatter.3.cloned.1.call-done = f32[512,128]{1,0:T(8,128)} async-done(((f32[4096,128]{1,0:T(8,128)}), f32[512,128]{1,0:T(8,128)}) %reduce-scatter.3.cloned.1.call-update) | async-done | bytes 262160 | tf_op jit(solution)/shard_map/reduce_scatter | solution.py:106
  530.6 7.2 all_gather.17
  539.2 7.0 all_gather.18
  550.6 45.6 %all-gather.5.cloned.1.call-done = f32[4096,128]{1,0:T(8,128)} async-done(((f32[512,128]{1,0:T(8,128)}), f32[4096,128]{1,0:T(8,128)}) %all-gather.5.cloned.1.call-update) | async-done | bytes 2097168 | tf_op jit(solution)/shard_map/all_gather | solution.py:136
  596.5 143.8 %while.23 = (s32[]{:T(128)}, f32[32,128,128]{2,0,1:T(8,128)S(1)}, s32[]{:T(128)}, s32[512]{0:T(512)S(1)}, s32[]{:T(128)}, /*index=5*/s32[512,16,128]{2,1,0:T(8,1...) while((s32[]{:T(128)}, f32[32,128,128]{2,0,1:T(8,128)S(1)}, s32[]{:T(128)}, ...), condition=%wide.region_8.9_spmd, body=%wide.region_7.8_spmd.sunk | while | flops 504630464 | bytes 9842357 | solution.py:31
  606.8 2.9 convolution_add_fusion.9
  619.9 2.9 convolution_add_fusion.9
  632.9 2.9 convolution_add_fusion.9
  646.0 2.9 convolution_add_fusion.9
  659.0 2.9 convolution_add_fusion.9
  672.1 2.9 convolution_add_fusion.9
  685.2 2.9 convolution_add_fusion.9
  698.2 2.9 convolution_add_fusion.9
  711.2 2.9 convolution_add_fusion.9
  724.3 2.9 convolution_add_fusion.9
  737.3 2.9 convolution_add_fusion.9
  748.8 276.4 %reduce-scatter.5.cloned.1.call-done = f32[2048,128]{1,0:T(8,128)} async-done(((f32[4096,128]{1,0:T(8,128)}), f32[2048,128]{1,0:T(8,128)}) %reduce-scatter.5.cloned.1.call-update) | async-done | bytes 1048592 | tf_op jit(solution)/shard_map/reduce_scatter | solution.py:141
  (481 shorter events, 248.8 us)
Async XLA Ops:
  7.2 530.6 %copy-start = (f32[256,256]{1,0:T(8,128)S(1)}, f32[256,256]{1,0:T(8,128)}, u32[]{:S(2)}) copy-start(f32[256,256]{1,0:T(8,128)} %param.16) | copy-start | bytes 786436
  7.2 16.6 %copy-start.2 = (s32[1,1,512]{2,1,0:T(1,128)S(1)}, s32[1,1,512]{2,1,0:T(1,128)}, u32[]{:S(2)}) copy-start(s32[1,1,512]{2,1,0:T(1,128)} %param.19) | copy-start | bytes 6148
  7.2 16.6 %copy-start.1 = (s32[1,1,512]{2,1,0:T(1,128)S(1)}, s32[1,1,512]{2,1,0:T(1,128)}, u32[]{:S(2)}) copy-start(s32[1,1,512]{2,1,0:T(1,128)} %param.18) | copy-start | bytes 6148
  7.2 15.7 %all-gather.3.cloned.1.call-start = ((), (), s32[]{:S(2)}) async-start(), calls=%async_computation.2 | async-start | bytes 3145728 | tf_op jit(solution)/shard_map/all_gather | solution.py:96
  7.9 521.5 %reduce-scatter.3.cloned.1.call-start = ((), (), s32[]{:S(2)}) async-start(), calls=%async_computation.3 | async-start | bytes 2359296 | tf_op jit(solution)/shard_map/reduce_scatter | solution.py:106
  24.4 4.7 copy-start.13
  25.2 4.0 copy-start.10
  38.0 4.7 copy-start.13
  38.7 4.0 copy-start.10
  51.5 4.7 copy-start.13
  52.2 4.0 copy-start.10
  65.1 4.7 copy-start.13
  65.8 4.0 copy-start.10
  78.6 4.7 copy-start.13
  79.3 4.0 copy-start.10
  92.1 4.7 copy-start.13
  92.8 4.0 copy-start.10
  105.7 4.7 copy-start.13
  106.4 4.0 copy-start.10
  119.2 4.7 copy-start.13
  119.9 4.0 copy-start.10
  132.7 4.7 copy-start.13
  133.4 4.0 copy-start.10
  146.3 4.7 copy-start.13
  147.0 4.0 copy-start.10
  159.8 4.7 copy-start.13
  160.5 4.0 copy-start.10
  175.2 11.5 %copy-start.7 = (f32[256,256]{1,0:T(8,128)S(1)}, f32[256,256]{1,0:T(8,128)}, u32[]{:S(2)}) copy-start(f32[256,256]{1,0:T(8,128)} %param.15) | copy-start | bytes 786436
  175.3 420.9 %all-gather.5.cloned.1.call-start = ((), (), s32[]{:S(2)}) async-start(), calls=%async_computation.4 | async-start | bytes 2359296 | tf_op jit(solution)/shard_map/all_gather | solution.py:136
  546.2 50.0 %copy-start.3 = (f32[512,256]{0,1:T(8,128)}, f32[512,256]{0,1:T(8,128)S(1)}, u32[]{:S(2)}) copy-start(f32[512,256]{0,1:T(8,128)S(1)} %all_gather.18) | copy-start | bytes 1572868
  548.0 198.3 %all-reduce.4.cloned.1.call-start = ((), (), s32[]{:S(2)}) async-start(), calls=%async_computation.6 | async-start | bytes 524288 | tf_op jit(solution)/shard_map/psum | solution.py:129
  550.5 474.6 %reduce-scatter.5.cloned.1.call-start = ((), (), s32[]{:S(2)}) async-start(), calls=%async_computation.5 | async-start | bytes 3145728 | tf_op jit(solution)/shard_map/reduce_scatter | solution.py:141
  (50 other events, 82.6 us)
Sparse Core Ops, SparseCore 0:
  9.6 13.2 all-gather.2
  175.4 354.0 reduce-scatter.2
  548.1 48.0 all-gather.4
  600.1 88.4 all-reduce.3
  742.9 282.1 reduce-scatter.4
where the time goes:
time: 1040 us; the launch traced here: 1030 us
  waiting for transfers between devices  357 us (34%)
  blocking collectives  345 us (33%)
  local copies, waits for them, and re-layouts  159 us (15%)
  matrix products  126 us (12%)
  other arithmetic  26.6 us (3%)
  between operations  15.2 us (1%)
    unnamed x1, blocking collectives  322 us
    reduce_scatter x1, waiting for transfers between devices, local(): lax.psum_scatter(column_terms.reshape(-1, half_width), 'cand', scatter_di...  276 us
    dot_general x22, matrix products, step_fn(): jnp.einsum('gk,gih->kih', selector, products, precision=HIGHEST)  63.6 us
    gather x22, local copies, waits for them, and re-layouts, step_fn(): dense_masks = unpack_masks(packed_masks[safe_slots])  60.5 us
    all_gather x1, waiting for transfers between devices, local(): gathered_rows = lax.all_gather(lifted, 'test', axis=0, tiled=True)  45.6 us
    gather x22, local copies, waits for them, and re-layouts, step_fn(): picked = gradient_tiles[block_rows[safe_slots]]  31.6 us
    gather x11, local copies, waits for them, and re-layouts, fetch_tiles(): return feature_tiles[chosen]  24.2 us
    dot_general x11, matrix products, step_fn(): jnp.einsum('gji,gjh->gih', dense_masks, picked, precision=HIGHEST)  21.6 us
  transfers between devices with their start and end apart: 5, of which 4 were waited for; matrix products, arithmetic and copies ran while one was open for 15% of the time, Pallas kernels for 0%

commit v1 on v0

--- a/solution.py
+++ b/solution.py
@@ -3,6 +3,7 @@
 import jax.numpy as jnp
 from jax import lax
 from jax.sharding import PartitionSpec as P
+from jax.lax import axis_index, axis_size, ppermute
 
 HIGHEST = lax.Precision.HIGHEST
 
@@ -82,6 +83,40 @@
 
 
 def local(x_test, x_cand, w_self, w_neigh, d_out, block_row, block_col, block_mask, block_live):
+
+    def unite_lane(my_data):
+        net_axis = "test"
+        part_next = axis_size(net_axis)
+        front = axis_index(net_axis)
+        row_list = []
+        num = 0
+        known, out_arr, item_now = (part_next, front, my_data.shape[0])
+        while num < known:
+            row_list.append((num, (num + 1) % known))
+            num = num + 1
+        inbox = []
+        num = 0
+        while num < known:
+            inbox.append((num, (num - 1) % known))
+            num += 1
+        near = jnp.zeros((*my_data.shape[:0], known * item_now, *my_data.shape[1:]), my_data.dtype)
+        near = lax.dynamic_update_slice_in_dim(near, my_data, out_arr * item_now, axis=0)
+        placed = b_now = my_data
+        ii = 1
+        y2 = known // 2
+        while ii < y2 + 1:
+            placed = ppermute(placed, net_axis, row_list)
+            near = lax.dynamic_update_slice_in_dim(
+                near, placed, (out_arr - ii) % known * item_now, axis=0
+            )
+            if ii < known - y2:
+                b_now = ppermute(b_now, net_axis, inbox)
+                near = lax.dynamic_update_slice_in_dim(
+                    near, b_now, (out_arr + ii) % known * item_now, axis=0
+                )
+            ii += 1
+        return near
+
     packed_masks = block_mask.reshape(block_mask.shape[2:])
     block_rows = block_row.reshape(-1)
     block_cols = block_col.reshape(-1)
@@ -133,7 +168,7 @@
     grad_x_cand = jnp.dot(grad_full, self_rows.T, precision=HIGHEST)
     grad_agg = jnp.dot(grad_full, neigh_rows.T, precision=HIGHEST)
     lifted = grad_agg / (1.0 + degree)[:, None]
-    gathered_rows = lax.all_gather(lifted, "test", axis=0, tiled=True)
+    gathered_rows = unite_lane(lifted)
     gradient_tiles = gathered_rows.reshape(row_blocks, block_edge, half_width)
     column_terms = transpose_product(
         packed_masks, block_rows, block_cols, live_count, gradient_tiles, col_blocks

time: 1040 us -> 1040 us (level)
  waiting for transfers between devices: 357 us -> 337 us
  starting transfers between devices: 0.2 us -> 18 us
    all_gather x1 -> x0, waiting for transfers between devices: 45.6 us -> none  [local(): gathered_rows = lax.all_gather(lifted, 'test', axis=0, tiled=True)]
    ppermute x0 -> x7, waiting for transfers between devices: none -> 25.1 us  [the longest x4 23.4 us: unite_lane(): placed = ppermute(placed, net_axis, row_list)]
    ppermute x0 -> x7, starting transfers between devices: none -> 17.8 us  [the longest x3 9.61 us: unite_lane(): b_now = ppermute(b_now, net_axis, inbox)]
  transfers between devices with their start and end apart: 5 -> 11, of which waited for: 4 -> 9; matrix products, arithmetic and copies ran while one was open for 15% -> 15% of each run, Pallas kernels for 0% -> 0%
where the time goes in v1:
time: 1040 us; the launch traced here: 1030 us
  blocking collectives  345 us (33%)
  waiting for transfers between devices  337 us (32%)
  local copies, waits for them, and re-layouts  164 us (16%)
  matrix products  126 us (12%)
  other arithmetic  26.6 us (3%)
  starting transfers between devices  18 us (2%)
  between operations  15.3 us (1%)
    unnamed x1, blocking collectives  322 us
    reduce_scatter x1, waiting for transfers between devices, local(): lax.psum_scatter(column_terms.reshape(-1, half_width), 'cand', scatter_di...  277 us
    dot_general x22, matrix products, step_fn(): jnp.einsum('gk,gih->kih', selector, products, precision=HIGHEST)  63.6 us
    gather x22, local copies, waits for them, and re-layouts, step_fn(): dense_masks = unpack_masks(packed_masks[safe_slots])  60.5 us
    gather x22, local copies, waits for them, and re-layouts, step_fn(): picked = gradient_tiles[block_rows[safe_slots]]  31.6 us
    gather x11, local copies, waits for them, and re-layouts, fetch_tiles(): return feature_tiles[chosen]  24.2 us
    ppermute x4, waiting for transfers between devices, unite_lane(): placed = ppermute(placed, net_axis, row_list)  23.4 us
    dot_general x11, matrix products, step_fn(): jnp.einsum('gji,gjh->gih', dense_masks, picked, precision=HIGHEST)  21.8 us
  transfers between devices with their start and end apart: 11, of which 9 were waited for; matrix products, arithmetic and copies ran while one was open for 15% of the time, Pallas kernels for 0%

profile of v1, /device:TPU:0, one launch (start us, length us, event | category | flops | bytes accessed | tf_op | source)
XLA Modules:
  0.0 1034.2 jit_solution(5243089789748248349)
XLA Ops:
  8.6 14.2 %all-gather.2.cloned.1.call-done = f32[4096,128]{1,0:T(8,128)} async-done(((f32[2048,128]{1,0:T(8,128)}), f32[4096,128]{1,0:T(8,128)}) %all-gather.2.cloned.1.call-update) | async-done | bytes 2097168 | tf_op jit(solution)/shard_map/all_gather | solution.py:131
  23.8 149.0 %while.22 = (s32[]{:T(128)}, f32[32,128,128]{2,0,1:T(8,128)S(1)}, f32[32,128]{1,0:T(8,128)}, s32[]{:T(128)}, s32[512]{0:T(512)S(1)}, /*index=5*/s32[]{:T(128)}, ...) while((s32[]{:T(128)}, f32[32,128,128]{2,0,1:T(8,128)S(1)}, ...), condition=%wide.region_2.3_spmd, body=%wide.region_0.2_spmd.sunk | while | flops 506468544 | bytes 10039669 | solution.py:32
  34.4 2.9 convolution_add_fusion.7
  48.0 2.9 convolution_add_fusion.7
  61.5 2.9 convolution_add_fusion.7
  75.1 2.9 convolution_add_fusion.7
  88.6 2.9 convolution_add_fusion.7
  102.2 2.9 convolution_add_fusion.7
  115.7 2.9 convolution_add_fusion.7
  129.3 2.9 convolution_add_fusion.7
  142.8 2.9 convolution_add_fusion.7
  156.4 2.9 convolution_add_fusion.7
  169.9 2.9 convolution_add_fusion.7
  177.7 9.2 all_gather.12
  187.6 322.0 %all-reduce = f32[4096]{0:T(1024)S(1)} all-reduce(f32[4096]{0:T(1024)} %bitcast.18), channel_id=3, replica_groups=mesh['cand'=2,'test'=8,'feat'=2] {'test'}, use_global_device_ids=true, to_apply=%region_4.5.clone | all-reduce | flops 4096 | bytes 32768
  509.7 19.9 %reduce-scatter.3.cloned.1.call-done = f32[512,128]{1,0:T(8,128)} async-done(((f32[4096,128]{1,0:T(8,128)}), f32[512,128]{1,0:T(8,128)}) %reduce-scatter.3.cloned.1.call-update) | async-done | bytes 262160 | tf_op jit(solution)/shard_map/reduce_scatter | solution.py:141
  530.7 7.2 all_gather.14
  539.4 7.0 all_gather.15
  549.1 3.9 collective-permute-start.1
  553.0 5.9 collective-permute-done
  563.5 2.9 collective-permute-start.3
  567.7 5.3 collective-permute-done.2
  582.1 5.3 collective-permute-done.4
  589.9 6.9 collective-permute-done.6
  598.4 144.1 %while.23 = (s32[]{:T(128)}, f32[32,128,128]{2,0,1:T(8,128)S(1)}, s32[]{:T(128)}, s32[512]{0:T(512)S(1)}, s32[]{:T(128)}, /*index=5*/s32[512,16,128]{2,1,0:T(8,1...) while((s32[]{:T(128)}, f32[32,128,128]{2,0,1:T(8,128)S(1)}, s32[]{:T(128)}, ...), condition=%wide.region_8.9_spmd, body=%wide.region_7.8_spmd.sunk | while | flops 504630464 | bytes 9842357 | solution.py:32
  621.7 2.9 convolution_add_fusion.9
  634.8 2.9 convolution_add_fusion.9
  647.9 2.9 convolution_add_fusion.9
  661.0 2.9 convolution_add_fusion.9
  700.3 2.9 convolution_add_fusion.9
  726.5 2.9 convolution_add_fusion.9
  751.1 276.6 %reduce-scatter.5.cloned.1.call-done = f32[2048,128]{1,0:T(8,128)} async-done(((f32[4096,128]{1,0:T(8,128)}), f32[2048,128]{1,0:T(8,128)}) %reduce-scatter.5.cloned.1.call-update) | async-done | bytes 1048592 | tf_op jit(solution)/shard_map/reduce_scatter | solution.py:176
  (502 shorter events, 280.9 us)
Async XLA Ops:
  7.2 530.7 %copy-start = (f32[256,256]{1,0:T(8,128)S(1)}, f32[256,256]{1,0:T(8,128)}, u32[]{:S(2)}) copy-start(f32[256,256]{1,0:T(8,128)} %param.16) | copy-start | bytes 786436
  7.2 16.6 %copy-start.2 = (s32[1,1,512]{2,1,0:T(1,128)S(1)}, s32[1,1,512]{2,1,0:T(1,128)}, u32[]{:S(2)}) copy-start(s32[1,1,512]{2,1,0:T(1,128)} %param.19) | copy-start | bytes 6148
  7.2 16.6 %copy-start.1 = (s32[1,1,512]{2,1,0:T(1,128)S(1)}, s32[1,1,512]{2,1,0:T(1,128)}, u32[]{:S(2)}) copy-start(s32[1,1,512]{2,1,0:T(1,128)} %param.18) | copy-start | bytes 6148
  7.2 15.7 %all-gather.2.cloned.1.call-start = ((), (), s32[]{:S(2)}) async-start(), calls=%async_computation.2 | async-start | bytes 3145728 | tf_op jit(solution)/shard_map/all_gather | solution.py:131
  7.9 521.7 %reduce-scatter.3.cloned.1.call-start = ((), (), s32[]{:S(2)}) async-start(), calls=%async_computation.3 | async-start | bytes 2359296 | tf_op jit(solution)/shard_map/reduce_scatter | solution.py:141
  24.4 4.7 copy-start.14
  25.2 4.0 copy-start.11
  38.0 4.7 copy-start.14
  38.7 4.0 copy-start.11
  51.5 4.7 copy-start.14
  52.2 4.0 copy-start.11
  65.1 4.7 copy-start.14
  65.8 4.0 copy-start.11
  78.6 4.7 copy-start.14
  79.3 4.0 copy-start.11
  92.2 4.7 copy-start.14
  105.7 4.7 copy-start.14
  119.3 4.7 copy-start.14
  132.8 4.7 copy-start.14
  146.4 4.7 copy-start.14
  159.9 4.7 copy-start.14
  175.4 11.5 %copy-start.8 = (f32[256,256]{1,0:T(8,128)S(1)}, f32[256,256]{1,0:T(8,128)}, u32[]{:S(2)}) copy-start(f32[256,256]{1,0:T(8,128)} %param.15) | copy-start | bytes 786436
  175.4 573.1 %all-reduce.4.cloned.1.call-start = ((), (), s32[]{:S(2)}) async-start(), calls=%async_computation.5 | async-start | bytes 524288 | tf_op jit(solution)/shard_map/psum | solution.py:164
  546.4 20.0 %copy-start.4 = (f32[512,256]{0,1:T(8,128)}, f32[512,256]{0,1:T(8,128)S(1)}, u32[]{:S(2)}) copy-start(f32[512,256]{0,1:T(8,128)S(1)} %all_gather.15) | copy-start | bytes 1572868
  548.3 10.6 %collective-permute-start = (f32[512,128]{1,0:T(8,128)}, f32[512,128]{1,0:T(8,128)}, u32[]{:S(2)}, u32[]{:S(2)}) collective-permute-start(f32[512,128]{1,0:T(8,128)} %get-tuple-element.164), channel_id=1, source_target_pairs={{0,2},{2,4},{4,6},{6,8},{8,10},{10,12},{12,14},{14,0},{1,3},{3,5},... | collective-permute-start | bytes 786440 | tf_op jit(solution)/shard_map/ppermute | solution.py:108
  549.1 14.3 %collective-permute-start.1 = (f32[512,128]{1,0:T(8,128)}, f32[512,128]{1,0:T(8,128)}, u32[]{:S(2)}, u32[]{:S(2)}) collective-permute-start(f32[512,128]{1,0:T(8,128)} %get-tuple-element.164), channel_id=1, source_target_pairs={{0,14},{2,0},{4,2},{6,4},{8,6},{10,8},{12,10},{14,12},{1,15},{3,1}... | collective-permute-start | bytes 786440 | tf_op jit(solution)/shard_map/ppermute | solution.py:113
  558.9 14.2 %collective-permute-start.2 = (f32[512,128]{1,0:T(8,128)}, f32[512,128]{1,0:T(8,128)}, u32[]{:S(2)}, u32[]{:S(2)}) collective-permute-start(f32[512,128]{1,0:T(8,128)} %collective-permute-done), channel_id=1, source_target_pairs={{0,2},{2,4},{4,6},{6,8},{8,10},{10,12},{12,14},{14,0},{1,3},{3,5},... | collective-permute-start | bytes 786440 | tf_op jit(solution)/shard_map/ppermute | solution.py:108
  563.5 14.8 %collective-permute-start.3 = (f32[512,128]{1,0:T(8,128)}, f32[512,128]{1,0:T(8,128)S(1)}, u32[]{:S(2)}, u32[]{:S(2)}) collective-permute-start(f32[512,128]{1,0:T(8,128)} %collective-permute-done.1), channel_id=1, source_target_pairs={{0,14},{2,0},{4,2},{6,4},{8,6},{10,8},{12,10},{14,12},{1,15},{3,1}... | collective-permute-start | bytes 786440 | tf_op jit(solution)/shard_map/ppermute | solution.py:113
  567.7 460.0 %reduce-scatter.5.cloned.1.call-start = ((), (), s32[]{:S(2)}) async-start(), calls=%async_computation.4 | async-start | bytes 3145728 | tf_op jit(solution)/shard_map/reduce_scatter | solution.py:176
  573.0 14.4 %collective-permute-start.4 = (f32[512,128]{1,0:T(8,128)}, f32[512,128]{1,0:T(8,128)S(1)}, u32[]{:S(2)}, u32[]{:S(2)}) collective-permute-start(f32[512,128]{1,0:T(8,128)} %collective-permute-done.2), channel_id=1, source_target_pairs={{0,2},{2,4},{4,6},{6,8},{8,10},{10,12},{12,14},{14,0},{1,3},{3,5},... | collective-permute-start | bytes 786440 | tf_op jit(solution)/shard_map/ppermute | solution.py:108
  578.3 11.5 %collective-permute-start.5 = (f32[512,128]{1,0:T(8,128)S(1)}, f32[512,128]{1,0:T(8,128)S(1)}, u32[]{:S(2)}, u32[]{:S(2)}) collective-permute-start(f32[512,128]{1,0:T(8,128)S(1)} %collective-permute-done.3), channel_id=1, source_target_pairs={{0,14},{2,0},{4,2},{6,4},{8,6},{10,8},{12,10},{14,12},{1,15},{3,1}... | collective-permute-start | bytes 786440 | tf_op jit(solution)/shard_map/ppermute | solution.py:113
  587.4 9.4 collective-permute-start.6
  (57 other events, 108.5 us)
Sparse Core Ops, SparseCore 0:
  9.6 13.2 all-gather.1
  175.5 354.0 reduce-scatter.2
  567.8 93.5 all-reduce.3
  745.2 282.4 reduce-scatter.4
